TPU v7x, 128 devices: a whole 4x4x4 slice. The times are simulated.
128 devices in a mesh: frow: 16 (over y, z), fcol: 8 (over x, core).
Axes of the slice: x: 4, y: 4, z: 4, core: 2. Of those that a mesh axis runs over, the one named last changes fastest.
Arguments:
- front_orig: float32 [16, 1024, 8, 2048], P('frow', None, 'fcol'), may hold values from -0.1 to 45, as said below
- child_tiles: bfloat16 [8192, 128, 128], P(('frow', 'fcol')), may hold values from -0.25 to 0.25
- tile_target: int32 [8192, 2], P(('frow', 'fcol')), may hold values from 0 to 127, as said below
- tile_rows: int32 [8192, 128], P(('frow', 'fcol')), may hold values from 0 to 127, each once within a row
- tile_cols: int32 [8192, 128], P(('frow', 'fcol')), may hold values from 0 to 127, each once within a row
Outputs:
- front_out: float32 [16, 1024, 8, 2048], P('frow', None, 'fcol')
Inputs may be any that keep to these rules, and one draw needn't show every extreme that they name: `front_orig`: Symmetric; the lower triangle of the front after every tile is added defines a positive definite matrix. `tile_target`: rows come 64 to a device in device order. Column 0 is the owner, frow index times 8 plus fcol index; column 1 the local block on that owner, local block row times 16 plus local block column; the block lies on or below the front's block diagonal. At most 2 tiles of one device go to one owner, and one owner receives exactly 2 from every device.
All inputs are finite; a program needn't handle non-finite values.
Results may differ from a plain program's by a relative error of at most 0.0003.
Values may be sent and summed in bfloat16 or wider, within the bound.
No kernel may reach another device: no remote copies, remote signals or barrier semaphores. Data moves between devices by JAX's collectives and lax.ppermute only.
A program may use at most 128 MiB of HBM per device.

v0:
```python
import jax
import jax.numpy as jnp
from jax import lax
from jax.sharding import PartitionSpec as P

PW = 512
NPANEL = 2
CAP = 2


def as_sent(x):
    return jax.tree.map(lambda a: a.astype(jnp.bfloat16) if a.dtype == jnp.float32 else a, x)


def broadcast(block, axis, source):
    block = jnp.where(lax.axis_index(axis) == source, block, jnp.zeros_like(block))
    return lax.psum(block, axis)


def place_tiles(received):
    tile_block, perm_block, target_block = received
    width = tile_block.shape[-1]
    positions = jnp.arange(width, dtype=jnp.int32)
    row_onehot = (perm_block[:, :, 0, None, :] == positions[:, None]).astype(jnp.bfloat16)
    col_onehot = (perm_block[:, :, 1, None, :] == positions[:, None]).astype(jnp.bfloat16)
    moved = jnp.einsum(
        "abxi,abij->abxj", row_onehot, tile_block, preferred_element_type=jnp.float32
    ).astype(jnp.bfloat16)
    placed = jnp.einsum(
        "abxj,abyj->abxy", moved, col_onehot, preferred_element_type=jnp.float32
    ).astype(jnp.bfloat16)
    return (placed, target_block)


def subtract_product(matrix, row_factor, col_factor):
    product = jnp.dot(
        row_factor,
        col_factor.T,
        precision=lax.Precision.HIGHEST,
        preferred_element_type=jnp.float32,
    )
    return matrix - product


def shards(front_orig, child_tiles, tile_target, tile_rows, tile_cols):
    row_devs = lax.axis_size("frow")
    col_devs = lax.axis_size("fcol")
    owners = row_devs * col_devs
    row_here = lax.axis_index("frow")
    col_here = lax.axis_index("fcol")
    width = child_tiles.shape[1]
    held = child_tiles.shape[0]
    slot_count = owners * CAP
    owner_of = tile_target[:, 0]
    block_of = tile_target[:, 1]
    tile_order = jnp.arange(held, dtype=jnp.int32)
    same_owner = owner_of[:, None] == owner_of[None, :]
    earlier = tile_order[None, :] < tile_order[:, None]
    rank_of = jnp.sum(jnp.where(same_owner & earlier, 1, 0), axis=1).astype(jnp.int32)
    slot_of = owner_of * CAP + rank_of
    slot_match = slot_of[None, :] == jnp.arange(slot_count, dtype=jnp.int32)[:, None]
    source_tile = jnp.sum(jnp.where(slot_match, tile_order[None, :], 0), axis=1)
    filled = jnp.any(slot_match, axis=1)
    send_tiles = jnp.where(
        filled[:, None, None],
        jnp.take(child_tiles, source_tile, axis=0),
        jnp.zeros((), jnp.bfloat16),
    )
    send_perms = jnp.stack(
        [jnp.take(tile_rows, source_tile, axis=0), jnp.take(tile_cols, source_tile, axis=0)], axis=1
    )
    send_blocks = jnp.take(block_of, source_tile, axis=0)
    placed, blocks_in = place_tiles(
        (
            lax.all_to_all(
                send_tiles.reshape(owners, CAP, width, width),
                ("frow", "fcol"),
                split_axis=0,
                concat_axis=0,
                tiled=True,
            ),
            lax.all_to_all(
                send_perms.reshape(owners, CAP, 2, width),
                ("frow", "fcol"),
                split_axis=0,
                concat_axis=0,
                tiled=True,
            ),
            lax.all_to_all(
                send_blocks.reshape(owners, CAP),
                ("frow", "fcol"),
                split_axis=0,
                concat_axis=0,
                tiled=True,
            ),
        )
    )
    local = front_orig[0, :, 0, :]
    row_blocks = local.shape[0] // width
    col_blocks = local.shape[1] // width
    block_ids = jnp.arange(row_blocks * col_blocks, dtype=jnp.int32)
    block_onehot = (blocks_in.reshape(1, slot_count) == block_ids[:, None]).astype(jnp.bfloat16)
    summed = jnp.dot(
        block_onehot, placed.reshape(slot_count, width * width), preferred_element_type=jnp.float32
    )
    added = (
        summed.reshape(row_blocks, col_blocks, width, width)
        .transpose(0, 2, 1, 3)
        .reshape(local.shape)
    )
    matrix = local + added
    local_rows = jnp.arange(local.shape[0], dtype=jnp.int32)
    local_cols = jnp.arange(local.shape[1], dtype=jnp.int32)
    global_rows = (local_rows // width * row_devs + row_here) * width + local_rows % width
    global_cols = (local_cols // width * col_devs + col_here) * width + local_cols % width
    total = NPANEL * PW
    hi = lax.Precision.HIGHEST
    row_panel = lax.all_gather(matrix[:, :width].astype(jnp.bfloat16), "fcol", axis=1, tiled=True)[
        :, :total
    ]
    half = row_devs // col_devs
    perms = []
    for shift in range(half):
        pairs = []
        for src_row in range(row_devs):
            for src_col in range(col_devs):
                part = src_row // col_devs
                dst_row = (part + shift) % half * col_devs + src_col
                dst_col = src_row % col_devs
                pairs.append((src_row * col_devs + src_col, dst_row * col_devs + dst_col))
        perms.append(pairs)
    got = [lax.ppermute(row_panel, ("frow", "fcol"), perm) for perm in perms]
    my_part = row_here // col_devs
    ordered = []
    for part in range(half):
        pick = got[0]
        for shift in range(1, half):
            pick = jnp.where((my_part - shift) % half == part, got[shift], pick)
        if half == 1:
            pick = got[0]
        ordered.append(pick.reshape(row_blocks, width, total))
    col_panel = jnp.stack(ordered, axis=1).reshape(local.shape[1], total)
    corner_blocks = total // width
    first = matrix[:width, :width].astype(jnp.bfloat16)
    every = lax.all_gather(first, ("frow", "fcol"), axis=0, tiled=False)
    every = every.reshape(row_devs, col_devs, width, width)[:corner_blocks, :corner_blocks]
    corner = every.transpose(0, 2, 1, 3).reshape(total, total).astype(jnp.float32)
    rows_all = jnp.concatenate([row_panel, col_panel], axis=0).astype(jnp.float32)
    n_own = local.shape[0]
    factor_full = jnp.zeros((total, total), jnp.float32)
    pieces = []
    eye = jnp.eye(PW, dtype=jnp.float32)
    for panel_idx in range(NPANEL):
        start = panel_idx * PW
        stop = start + PW
        diag_block = corner[start:stop, start:stop]
        symmetric = jnp.tril(diag_block) + jnp.tril(diag_block, -1).T
        factor = jnp.linalg.cholesky(symmetric)
        inverse = lax.linalg.triangular_solve(factor, eye, left_side=True, lower=True)
        factor_full = factor_full.at[start:stop, start:stop].set(factor)
        solved_rows = jnp.dot(
            rows_all[:, start:stop], inverse.T, precision=hi, preferred_element_type=jnp.float32
        )
        pieces.append(solved_rows)
        if stop < total:
            below = jnp.dot(
                corner[stop:, start:stop],
                inverse.T,
                precision=hi,
                preferred_element_type=jnp.float32,
            )
            factor_full = factor_full.at[stop:, start:stop].set(below)
            corner = corner.at[stop:, stop:].add(
                -jnp.dot(below, below.T, precision=hi, preferred_element_type=jnp.float32)
            )
            rows_all = rows_all.at[:, stop:].add(
                -jnp.dot(solved_rows, below.T, precision=hi, preferred_element_type=jnp.float32)
            )
    solved = jnp.concatenate(pieces, axis=1)
    row_factor = solved[:n_own]
    col_factor = solved[n_own:]
    matrix = subtract_product(matrix, row_factor, col_factor)
    in_corner = (global_rows < total)[:, None]
    corner_rows = jnp.take(factor_full, jnp.clip(global_rows, 0, total - 1), axis=0)
    panel_vals = jnp.where(in_corner, corner_rows, row_factor)
    own_part = lax.dynamic_slice_in_dim(panel_vals, col_here * width, width, axis=1)
    matrix = matrix.at[:, :width].set(own_part)
    lower_part = global_rows[:, None] >= global_cols[None, :]
    result = jnp.where(lower_part, matrix, 0.0)
    return result[None, :, None, :]


def solution(mesh):
    return jax.shard_map(
        shards,
        mesh=mesh,
        in_specs=(
            P("frow", None, "fcol", None),
            P(("frow", "fcol"), None, None),
            P(("frow", "fcol"), None),
            P(("frow", "fcol"), None),
            P(("frow", "fcol"), None),
        ),
        out_specs=P("frow", None, "fcol", None),
        check_vma=False,
    )
```

profile of v0, /device:TPU:1, one launch (start us, length us, event | category | flops | bytes accessed | tf_op | source)
XLA Modules:
  0.0 974.5 jit_solution(10013576491422661252)
XLA Ops:
  11.2 11.5 %all-to-all-start = ((s32[128,1,2]{2,1,0:T(1,128)}), s32[128,1,2]{2,1,0:T(1,128)S(1)}, u32[]{:S(2)}, u32[]{:S(2)}) async-start(s32[128,1,2]{2,1,0:T(1,128)} %bitcast.5), calls=%async_computation | async-start | bytes 131072 | tf_op jit(solution)/shard_map/all_to_all | solution.py:89
  27.0 8.6 gather_fusion.1
  35.6 9.8 %all-to-all-start.1 = ((s32[128,2,2,128]{3,1,2,0:T(2,128)}), s32[128,2,2,128]{3,1,2,0:T(2,128)S(1)}, u32[]{:S(2)}, u32[]{:S(2)}) async-start(s32[128,2,2,128]{3,1,2,0:T(2,128)} %pad_add_fusion), calls=%async_computation.1 | async-start | bytes 524288 | tf_op jit(solution)/shard_map/all_to_all | solution.py:82
  45.3 7.4 select_select_fusion
  52.8 3.5 all-to-all-done.1
  56.3 6.7 all-to-all-start.2
  63.1 20.7 %copy.55 = f32[1,1024,1,2048]{1,3,2,0:T(8,128)} copy(f32[1,1024,1,2048]{3,2,1,0:T(1,128)} %param.22) | data formatting | bytes 16777216 | tf_op args[0]
  85.3 78.3 %all-to-all-done.2 = bf16[128,2,128,128]{3,2,1,0:T(8,128)(2,1)} async-done(((bf16[128,2,128,128]{3,2,1,0:T(8,128)(2,1)}), bf16[128,2,128,128]{3,2,1,0:T(8,128)(2,1)}, u32[]{:S(2)}, u32[]{:S(2)}) %all-to-all-start.2) | async-done | bytes 8388640 | tf_op jit(solution)/shard_map/all_to_all | solution.py:75
  163.6 13.1 %fusion.8 = bf16[128,2,128,128]{3,2,1,0:T(8,128)(2,1)} fusion(s32[128,2,128]{2,1,0:T(2,128)S(1)} %get-tuple-element.125, bf16[128,2,128,128]{3,2,1,0:T(8,128)(2,1)} %all-to-all-done.2, s32[128,2,128]{2,1,0:T(2,128)S(1)} %get-tuple-element.124), kind=kOutput, calls=%fused_computation.24 | convolution fusion | flops 2164260864 | bytes 17039360 | tf_op jit(solution)/shard_map/abxj,abyj->abxy/dot_general | solution.py:29
  176.8 35.1 %copy.100 = bf16[32,8,128,128]{3,1,2,0:T(8,128)(2,1)} copy(bf16[32,8,128,128]{3,2,1,0:T(8,128)(2,1)} %bitcast.180) | data formatting | bytes 16777216
  211.9 11.9 %copy.59 = bf16[16384,256]{1,0:T(8,128)(2,1)} copy(bf16[16384,256]{0,1:T(8,128)(2,1)} %bitcast.176) | data formatting | bytes 16777216 | tf_op jit(solution)/shard_map/dot_general | solution.py:103
  223.8 6.2 fusion.83
  230.0 7.5 copy.99
  237.5 9.2 copy.60
  246.8 7.3 fusion.17
  258.3 28.5 %all-gather.4.cloned.1.call-done = bf16[1024,1024]{0,1:T(8,128)(2,1)} async-done(((bf16[1024,128]{0,1:T(8,128)(2,1)}), bf16[1024,1024]{0,1:T(8,128)(2,1)}) %all-gather.4.cloned.1.call-update) | async-done | bytes 2097168 | tf_op jit(solution)/shard_map/all_gather | solution.py:118
  286.8 3.3 collective-permute-start.1
  290.1 2.9 collective-permute-start
  296.2 3.9 copy.63
  300.1 37.2 %collective-permute-done.1 = bf16[1024,1024]{0,1:T(8,128)(2,1)} collective-permute-done((bf16[1024,1024]{0,1:T(8,128)(2,1)}, bf16[1024,1024]{0,1:T(8,128)(2,1)}, u32[]{:S(2)}, u32[]{:S(2)}) %collective-permute-start.1) | collective-permute-done | bytes 2097184 | tf_op jit(solution)/shard_map/ppermute | solution.py:132
  337.2 137.8 %collective-permute-done = bf16[1024,1024]{0,1:T(8,128)(2,1)} collective-permute-done((bf16[1024,1024]{0,1:T(8,128)(2,1)}, bf16[1024,1024]{0,1:T(8,128)(2,1)}, u32[]{:S(2)}, u32[]{:S(2)}) %collective-permute-start) | collective-permute-done | bytes 2097184 | tf_op jit(solution)/shard_map/ppermute | solution.py:132
  475.0 4.5 broadcast_select_fusion.1
  479.5 3.9 copy.76
  483.4 4.0 copy.77
  487.4 4.6 pad_maximum_fusion.2
  492.1 29.1 %all-gather.6.cloned.1.call-done = bf16[16384,128]{0,1:T(8,128)(2,1)} async-done(((bf16[128,128]{0,1:T(8,128)(2,1)}), bf16[16384,128]{0,1:T(8,128)(2,1)}) %all-gather.6.cloned.1.call-update) | async-done | bytes 4194320 | tf_op jit(solution)/shard_map/all_gather | solution.py:145
  524.8 4.9 copy.64
  529.7 3.7 copy_bitcast_fusion.1
  538.8 11.7 %cholesky.286 = f32[128,128]{1,0:T(8,128)S(1)} custom-call(f32[128,128]{1,0:T(8,128)S(1)} %cholesky.426), custom_call_target="Cholesky" | custom-call | tf_op jit(solution)/shard_map/jit(cholesky)/cholesky | solution.py:158
  550.6 9.8 %custom-call.27 = f32[1,128,128]{1,2,0:T(8,128)S(1)} custom-call(f32[1,128,128]{2,1,0:T(8,128)S(1)} %get-tuple-element.145), custom_call_target="InvertDiagBlocksLowerTriangular" | custom-call | tf_op jit(solution)/shard_map/jit(cholesky)/cholesky | solution.py:158
  563.0 11.7 %cholesky.305 = f32[128,128]{1,0:T(8,128)S(1)} custom-call(f32[128,128]{1,0:T(8,128)S(1)} %cholesky.430), custom_call_target="Cholesky" | custom-call | tf_op jit(solution)/shard_map/jit(cholesky)/cholesky | solution.py:158
  574.8 10.0 %custom-call.28 = f32[1,128,128]{1,2,0:T(8,128)S(1)} custom-call(f32[1,128,128]{2,1,0:T(8,128)S(1)} %get-tuple-element.142), custom_call_target="InvertDiagBlocksLowerTriangular" | custom-call | tf_op jit(solution)/shard_map/jit(cholesky)/cholesky | solution.py:158
  586.3 11.7 %cholesky.326 = f32[128,128]{1,0:T(8,128)S(1)} custom-call(f32[128,128]{1,0:T(8,128)S(1)} %cholesky.435), custom_call_target="Cholesky" | custom-call | tf_op jit(solution)/shard_map/jit(cholesky)/cholesky | solution.py:158
  598.7 9.8 %custom-call.29 = f32[1,128,128]{1,2,0:T(8,128)S(1)} custom-call(f32[1,128,128]{2,1,0:T(8,128)S(1)} %get-tuple-element.139), custom_call_target="InvertDiagBlocksLowerTriangular" | custom-call | tf_op jit(solution)/shard_map/jit(cholesky)/cholesky | solution.py:158
  610.0 12.1 %cholesky.343 = f32[128,128]{1,0:T(8,128)S(1)} custom-call(f32[128,128]{1,0:T(8,128)S(1)} %convolution_subtract_fusion.11), custom_call_target="Cholesky" | custom-call | tf_op jit(solution)/shard_map/jit(cholesky)/cholesky | solution.py:158
  627.0 11.6 %while.10 = (s32[]{:T(128)}, f32[512,512]{1,0:T(8,128)}, s32[4,2]{0,1:T(2,128)S(1)}, f32[4,128,128]{2,1,0:T(8,128)S(1)}, s32[]{:T(128)}) while((s32[]{:T(128)}, f32[512,512]{1,0:T(8,128)}, s32[4,2]{0,1:T(2,128)S(1)}, f32[4,128,128]{2,1,0:T(8,128)S(1)}, s32[]{:T(128)}) %tuple.86), condition=%wide.while_cond.6, body=%wide.while_body.6.sunk | while | flops 2 | bytes 131189 | solution.py:159
  627.7 2.2 bitcast_dynamic-update-slice_fusion.4
  630.6 2.2 bitcast_dynamic-update-slice_fusion.4
  633.5 2.2 bitcast_dynamic-update-slice_fusion.4
  638.6 39.3 %custom-call.30 = f32[4,128,128]{1,2,0:T(8,128)S(1)} custom-call(f32[4,128,128]{2,1,0:T(8,128)S(1)} %get-tuple-element.94), custom_call_target="InvertDiagBlocksLowerTriangular" | custom-call | tf_op jit(solution)/shard_map/triangular_solve/custom-call.3 | solution.py:159
  683.9 2.5 scatter.14
  686.5 3.1 constant_dynamic-update-slice_fusion.4
  689.6 4.1 broadcast_select_fusion.2
  700.5 11.7 %cholesky.358 = f32[128,128]{1,0:T(8,128)S(1)} custom-call(f32[128,128]{1,0:T(8,128)S(1)} %cholesky.439), custom_call_target="Cholesky" | custom-call | tf_op jit(solution)/shard_map/jit(cholesky)/cholesky | solution.py:158
  713.0 10.0 %custom-call.31 = f32[1,128,128]{1,2,0:T(8,128)S(1)} custom-call(f32[1,128,128]{2,1,0:T(8,128)S(1)} %get-tuple-element.135), custom_call_target="InvertDiagBlocksLowerTriangular" | custom-call | tf_op jit(solution)/shard_map/jit(cholesky)/cholesky | solution.py:158
  726.3 11.7 %cholesky.377 = f32[128,128]{1,0:T(8,128)S(1)} custom-call(f32[128,128]{1,0:T(8,128)S(1)} %cholesky.443), custom_call_target="Cholesky" | custom-call | tf_op jit(solution)/shard_map/jit(cholesky)/cholesky | solution.py:158
  738.7 9.8 %custom-call.32 = f32[1,128,128]{1,2,0:T(8,128)S(1)} custom-call(f32[1,128,128]{2,1,0:T(8,128)S(1)} %get-tuple-element.132), custom_call_target="InvertDiagBlocksLowerTriangular" | custom-call | tf_op jit(solution)/shard_map/jit(cholesky)/cholesky | solution.py:158
  751.6 11.7 %cholesky.398 = f32[128,128]{1,0:T(8,128)S(1)} custom-call(f32[128,128]{1,0:T(8,128)S(1)} %cholesky.448), custom_call_target="Cholesky" | custom-call | tf_op jit(solution)/shard_map/jit(cholesky)/cholesky | solution.py:158
  764.0 10.0 %custom-call.33 = f32[1,128,128]{1,2,0:T(8,128)S(1)} custom-call(f32[1,128,128]{2,1,0:T(8,128)S(1)} %get-tuple-element.129), custom_call_target="InvertDiagBlocksLowerTriangular" | custom-call | tf_op jit(solution)/shard_map/jit(cholesky)/cholesky | solution.py:158
  776.3 11.7 %cholesky.415 = f32[128,128]{1,0:T(8,128)S(1)} custom-call(f32[128,128]{1,0:T(8,128)S(1)} %convolution_subtract_fusion.10), custom_call_target="Cholesky" | custom-call | tf_op jit(solution)/shard_map/jit(cholesky)/cholesky | solution.py:158
  792.8 8.8 gather_fusion.2
  805.6 11.8 %while.11 = (s32[]{:T(128)}, f32[512,512]{1,0:T(8,128)}, s32[4,2]{0,1:T(2,128)S(1)}, f32[4,128,128]{2,1,0:T(8,128)S(1)}, s32[]{:T(128)}) while((s32[]{:T(128)}, f32[512,512]{1,0:T(8,128)}, s32[4,2]{0,1:T(2,128)S(1)}, f32[4,128,128]{2,1,0:T(8,128)S(1)}, s32[]{:T(128)}) %tuple.96), condition=%wide.while_cond.6.clone, body=%wide.while_body.6.clone.sunk | while | flops 2 | bytes 131189 | solution.py:159
  806.3 2.3 bitcast_dynamic-update-slice_fusion.5
  809.2 2.3 bitcast_dynamic-update-slice_fusion.5
  812.2 2.3 bitcast_dynamic-update-slice_fusion.5
  815.2 2.2 bitcast_dynamic-update-slice_fusion.5
  817.4 39.7 %custom-call.34 = f32[4,128,128]{1,2,0:T(8,128)S(1)} custom-call(f32[4,128,128]{2,1,0:T(8,128)S(1)} %get-tuple-element.95), custom_call_target="InvertDiagBlocksLowerTriangular" | custom-call | tf_op jit(solution)/shard_map/triangular_solve/custom-call.3 | solution.py:159
  866.4 7.0 fusion.21
  873.5 21.5 %fusion.149 = f32[3072,512]{1,0:T(8,128)S(1)} fusion(f32[3072,512]{0,1:T(8,128)S(1)} %fusion.21, f32[512,512]{1,0:T(8,128)S(1)} %get-tuple-element.153), kind=kOutput, calls=%fused_computation.282 | convolution fusion | flops 9663676416 | bytes 13631488 | tf_op jit(solution)/shard_map/dot_general | solution.py:177
  895.0 12.4 %fusion.11 = f32[3072,512]{0,1:T(8,128)S(1)} fusion(f32[3072,512]{1,0:T(8,128)S(1)} %fusion.149, bf16[2048,1024]{1,0:T(8,128)(2,1)} %bitcast.179, bf16[1024,1024]{1,0:T(8,128)(2,1)S(1)} %copy-done.3, f32[128,512]{1,0:T(8,128)S(1)} %fusion.86, f32[128,512]{1,0:T(8,128)S(1)} %copy-done.12, f32[128,512]{1,0:T(8,128)S(1)} %copy-done.6, f32[128,512]{1,0:T(8,128)S(1)} %fusion.65), kind=kOutput, calls=%fused_computation.27 | convolution fusion | flops 9673900032 | bytes 19922944 | tf_op jit(solution)/shard_map/dot_general | solution.py:161
  907.5 30.5 %fusion.16 = f32[1024,2048]{0,1:T(8,128)} fusion(f32[1024,2048]{0,1:T(8,128)} %copy.60, f32[1,1024,1,2048]{1,3,2,0:T(8,128)S(1)} %bitcast.174, f32[3072,512]{0,1:T(8,128)S(1)} %fusion.11, f32[3072,512]{0,1:T(8,128)S(1)} %fusion.21), kind=kOutput, calls=%fused_computation.33 | convolution fusion | flops 25777143808 | bytes 37748736 | tf_op jit(solution)/shard_map/dot_general | solution.py:36
  938.0 2.8 fusion.55
  940.8 5.9 select_bitcast_fusion
  946.8 20.5 %copy.73 = f32[1,1024,1,2048]{3,2,1,0:T(1,128)} copy(f32[1,1024,1,2048]{1,3,2,0:T(8,128)} %select_bitcast_fusion) | data formatting | bytes 16777216 | tf_op jit(solution)/shard_map/broadcast_in_dim | solution.py:190
  (179 shorter events, 82.2 us)
Async XLA Ops:
  6.5 20.5 %copy-start = (bf16[64,128,128]{2,1,0:T(8,128)(2,1)S(1)}, bf16[64,128,128]{2,1,0:T(8,128)(2,1)}, u32[]{:S(2)}) copy-start(bf16[64,128,128]{2,1,0:T(8,128)(2,1)} %param.23) | copy-start | bytes 6291460
  11.2 24.4 %all-to-all-start = ((s32[128,1,2]{2,1,0:T(1,128)}), s32[128,1,2]{2,1,0:T(1,128)S(1)}, u32[]{:S(2)}, u32[]{:S(2)}) async-start(s32[128,1,2]{2,1,0:T(1,128)} %bitcast.5), calls=%async_computation | async-start | bytes 131072 | tf_op jit(solution)/shard_map/all_to_all | solution.py:89
  35.6 20.7 %all-to-all-start.1 = ((s32[128,2,2,128]{3,1,2,0:T(2,128)}), s32[128,2,2,128]{3,1,2,0:T(2,128)S(1)}, u32[]{:S(2)}, u32[]{:S(2)}) async-start(s32[128,2,2,128]{3,1,2,0:T(2,128)} %pad_add_fusion), calls=%async_computation.1 | async-start | bytes 524288 | tf_op jit(solution)/shard_map/all_to_all | solution.py:82
  56.3 107.4 %all-to-all-start.2 = ((bf16[128,2,128,128]{3,2,1,0:T(8,128)(2,1)}), bf16[128,2,128,128]{3,2,1,0:T(8,128)(2,1)}, u32[]{:S(2)}, u32[]{:S(2)}) async-start(bf16[128,2,128,128]{3,2,1,0:T(8,128)(2,1)} %select_select_fusion), calls=%async_computation.2 | async-start | bytes 16777216 | tf_op jit(solution)/shard_map/all_to_all | solution.py:75
  63.0 223.8 %all-gather.4.cloned.1.call-start = ((), (), s32[]{:S(2)}) async-start(), calls=%async_computation.3 | async-start | bytes 2359296 | tf_op jit(solution)/shard_map/all_gather | solution.py:118
  254.1 2.0 copy-start.4
  256.8 264.3 %all-gather.6.cloned.1.call-start = ((), (), s32[]{:S(2)}) async-start(), calls=%async_computation.4 | async-start | bytes 4227072 | tf_op jit(solution)/shard_map/all_gather | solution.py:145
  286.8 50.5 %collective-permute-start.1 = (bf16[1024,1024]{0,1:T(8,128)(2,1)}, bf16[1024,1024]{0,1:T(8,128)(2,1)}, u32[]{:S(2)}, u32[]{:S(2)}) collective-permute-start(bf16[1024,1024]{0,1:T(8,128)(2,1)} %all-gather.4.cloned.1.call-done), channel_id=1, source_target_pairs={{0,0},{1,8},{2,16},{3,24},{4,32},{5,40},{6,48},{7,56},{8,1},{9,9},... | collective-permute-start | bytes 6291464 | tf_op jit(solution)/shard_map/ppermute | solution.py:132
  290.1 184.9 %collective-permute-start = (bf16[1024,1024]{0,1:T(8,128)(2,1)}, bf16[1024,1024]{0,1:T(8,128)(2,1)}, u32[]{:S(2)}, u32[]{:S(2)}) collective-permute-start(bf16[1024,1024]{0,1:T(8,128)(2,1)} %all-gather.4.cloned.1.call-done), channel_id=1, source_target_pairs={{0,64},{1,72},{2,80},{3,88},{4,96},{5,104},{6,112},{7,120},{8,65},... | collective-permute-start | bytes 6291464 | tf_op jit(solution)/shard_map/ppermute | solution.py:132
  533.4 1.9 copy-start.2
  537.8 1.0 copy-start.10
  680.0 9.6 copy-start.7
  680.0 9.6 copy-start.17
  681.8 11.9 %copy-start.13 = (f32[128,512]{1,0:T(8,128)}, f32[128,512]{1,0:T(8,128)S(1)}, u32[]{:S(2)}) copy-start(f32[128,512]{1,0:T(8,128)S(1)} %fusion.93) | copy-start | bytes 786436
  683.9 9.8 %copy-start.16 = (f32[128,512]{1,0:T(8,128)}, f32[128,512]{1,0:T(8,128)S(1)}, u32[]{:S(2)}) copy-start(f32[128,512]{1,0:T(8,128)S(1)} %fusion.92) | copy-start | bytes 786436
  699.5 1.0 copy-start.9
  725.6 0.7 copy-start.18
  751.0 0.7 copy-start.19
  801.6 64.8 %copy-start.8 = (f32[128,512]{1,0:T(8,128)S(1)}, f32[128,512]{1,0:T(8,128)}, u32[]{:S(2)}) copy-start(f32[128,512]{1,0:T(8,128)} %copy-done.7) | copy-start | bytes 786436
  801.6 64.8 %copy-start.14 = (f32[128,512]{1,0:T(8,128)S(1)}, f32[128,512]{1,0:T(8,128)}, u32[]{:S(2)}) copy-start(f32[128,512]{1,0:T(8,128)} %copy-done.13) | copy-start | bytes 786436
  857.1 0.7 copy-start.20
  860.7 5.6 copy-start.5
  863.4 2.9 copy-start.11
  873.4 21.5 %copy-start.3 = (bf16[1024,1024]{1,0:T(8,128)(2,1)S(1)}, bf16[1024,1024]{1,0:T(8,128)(2,1)}, u32[]{:S(2)}) copy-start(bf16[1024,1024]{1,0:T(8,128)(2,1)} %copy.63) | copy-start | bytes 6291460
  873.4 21.5 %copy-start.6 = (f32[128,512]{1,0:T(8,128)S(1)}, f32[128,512]{1,0:T(8,128)}, u32[]{:S(2)}) copy-start(f32[128,512]{1,0:T(8,128)} %copy-done.5) | copy-start | bytes 786436
  873.5 21.5 %copy-start.12 = (f32[128,512]{1,0:T(8,128)S(1)}, f32[128,512]{1,0:T(8,128)}, u32[]{:S(2)}) copy-start(f32[128,512]{1,0:T(8,128)} %copy-done.11) | copy-start | bytes 786436
  873.5 34.0 %slice-start = ((s8[8388608]{0:T(1024)(128)(4,1)}), s8[4194304]{0:T(1024)(128)(4,1)S(1)}, s32[]{:S(2)}) async-start(s8[8388608]{0:T(1024)(128)(4,1)} %bitcast.173), calls=%async_computation.5 | async-start | bytes 8388608
  895.0 12.4 %slice-start.1 = ((s8[8388608]{0:T(1024)(128)(4,1)}), s8[4194304]{0:T(1024)(128)(4,1)S(1)}, s32[]{:S(2)}) async-start(s8[8388608]{0:T(1024)(128)(4,1)} %bitcast.173), calls=%async_computation.6 | async-start | bytes 8388608
  907.5 30.6 %copy-start.15 = (f32[1024,128]{0,1:T(8,128)S(1)}, f32[1024,128]{0,1:T(8,128)}, u32[]{:S(2)}) copy-start(f32[1024,128]{0,1:T(8,128)} %copy.89) | copy-start | bytes 1572868
  907.5 30.5 %copy-start.21 = (pred[1024]{0:T(1024)(128)(4,1)S(1)}, pred[1024]{0:T(1024)(128)(4,1)}, u32[]{:S(2)}) copy-start(pred[1024]{0:T(1024)(128)(4,1)} %get-tuple-element.158) | copy-start | bytes 3076
  907.5 30.5 %copy-start.22 = (pred[1024]{0:T(1024)(128)(4,1)S(1)}, pred[1024]{0:T(1024)(128)(4,1)}, u32[]{:S(2)}) copy-start(pred[1024]{0:T(1024)(128)(4,1)} %get-tuple-element.159) | copy-start | bytes 3076
  940.8 26.4 %copy-start.1 = (bf16[64,128,128]{2,1,0:T(8,128)(2,1)S(1)}, bf16[64,128,128]{2,1,0:T(8,128)(2,1)}, u32[]{:S(2)}) copy-start(bf16[64,128,128]{2,1,0:T(8,128)(2,1)} %param.23) | copy-start | bytes 6291460
Sparse Core Ops, SparseCore 0:
  256.9 29.7 all-gather.3
  289.6 231.5 all-gather.5
where the time goes:
time: 987 us; the launch traced here: 975 us
  waiting for transfers between devices  314 us (32%)
  other arithmetic  287 us (29%)
  local copies, waits for them, and re-layouts  194 us (20%)
  matrix products  125 us (13%)
  starting transfers between devices  34.3 us (3%)
  between operations  19.6 us (2%)
    ppermute x2, waiting for transfers between devices, shards(): got = [lax.ppermute(row_panel, ('frow', 'fcol'), perm) for perm in perms]  175 us
    another operation x29, other arithmetic, shards(): factor = jnp.linalg.cholesky(symmetric)  158 us
    another operation x4, other arithmetic, shards(): lax.linalg.triangular_solve(factor, eye, left_side=True, lower=True)  80.3 us
    all_to_all x1, waiting for transfers between devices, shards(): lax.all_to_all(send_tiles.reshape(owners, CAP, width, width), ('frow', 'f...  78.3 us
    unnamed x56, local copies, waits for them, and re-layouts  77 us
    dot_general x1, matrix products, subtract_product(): jnp.dot(row_factor, col_factor.T, precision=lax.Precision.HIGHEST, prefer...  30.5 us
    all_gather x1, waiting for transfers between devices, shards(): every = lax.all_gather(first, ('frow', 'fcol'), axis=0, tiled=False)  29.1 us
    all_gather x1, waiting for transfers between devices, shards(): lax.all_gather(matrix[:, :width].astype(jnp.bfloat16), 'fcol', axis=1, ti...  28.5 us
  transfers between devices with their start and end apart: 7, of which 6 were waited for; matrix products, arithmetic and copies ran while one was open for 7% of the time, Pallas kernels for 0%

commit v1 on v0

--- a/solution.py
+++ b/solution.py
@@ -1,3 +1,4 @@
+import functools
 import jax
 import jax.numpy as jnp
 from jax import lax
@@ -6,6 +7,16 @@
 PW = 512
 NPANEL = 2
 CAP = 2
+
+
+def pair_things_for(inner_x, bus_axis):
+    u1 = lax.axis_size(bus_axis)
+    built = jnp.stack(u1 * [inner_x], 0)
+    lower = lax.all_to_all(built, axis_name=bus_axis, split_axis=0, concat_axis=0)
+    return jnp.concatenate(lower, 1)
+
+
+end_leaves = functools.partial(pair_things_for, bus_axis="fcol")
 
 
 def as_sent(x):
@@ -115,9 +126,7 @@
     global_cols = (local_cols // width * col_devs + col_here) * width + local_cols % width
     total = NPANEL * PW
     hi = lax.Precision.HIGHEST
-    row_panel = lax.all_gather(matrix[:, :width].astype(jnp.bfloat16), "fcol", axis=1, tiled=True)[
-        :, :total
-    ]
+    row_panel = end_leaves(matrix[:, :width].astype(jnp.bfloat16))[:, :total]
     half = row_devs // col_devs
     perms = []
     for shift in range(half):

time: 987 us -> 977 us (0.990)
  waiting for transfers between devices: 314 us -> 267 us
  blocking collectives: 0 us -> 34 us
    all_to_all x0 -> x1, blocking collectives: none -> 34 us  [pair_things_for(): lax.all_to_all(built, axis_name=bus_axis, split_axis=0, concat_axis=0)]
    all_gather x1 -> x0, waiting for transfers between devices: 28.5 us -> none  [shards(): lax.all_gather(matrix[:, :width].astype(jnp.bfloat16), 'fcol', axis=1, ti...]
    all_gather x1, waiting for transfers between devices: 29.1 us -> 10.9 us  [shards(): every = lax.all_gather(first, ('frow', 'fcol'), axis=0, tiled=False)]
  transfers between devices with their start and end apart: 7 -> 6, of which waited for: 6 -> 5; matrix products, arithmetic and copies ran while one was open for 7% -> 7% of each run, Pallas kernels for 0% -> 0%
where the time goes in v1:
time: 977 us; the launch traced here: 964 us
  other arithmetic  287 us (29%)
  waiting for transfers between devices  267 us (27%)
  local copies, waits for them, and re-layouts  195 us (20%)
  matrix products  125 us (13%)
  starting transfers between devices  36.1 us (4%)
  blocking collectives  34 us (3%)
  between operations  19.9 us (2%)
    ppermute x2, waiting for transfers between devices, shards(): got = [lax.ppermute(row_panel, ('frow', 'fcol'), perm) for perm in perms]  175 us
    another operation x29, other arithmetic, shards(): factor = jnp.linalg.cholesky(symmetric)  159 us
    another operation x4, other arithmetic, shards(): lax.linalg.triangular_solve(factor, eye, left_side=True, lower=True)  80.3 us
    all_to_all x1, waiting for transfers between devices, shards(): lax.all_to_all(send_tiles.reshape(owners, CAP, width, width), ('frow', 'f...  78.2 us
    unnamed x56, local copies, waits for them, and re-layouts  77.1 us
    all_to_all x1, blocking collectives, pair_things_for(): lax.all_to_all(built, axis_name=bus_axis, split_axis=0, concat_axis=0)  34 us
    dot_general x1, matrix products, subtract_product(): jnp.dot(row_factor, col_factor.T, precision=lax.Precision.HIGHEST, prefer...  30.5 us
    another operation x27, local copies, waits for them, and re-layouts, shards(): lax.linalg.triangular_solve(factor, eye, left_side=True, lower=True)  23.6 us
  transfers between devices with their start and end apart: 6, of which 5 were waited for; matrix products, arithmetic and copies ran while one was open for 7% of the time, Pallas kernels for 0%

profile of v1, /device:TPU:1, one launch (start us, length us, event | category | flops | bytes accessed | tf_op | source)
XLA Modules:
  0.0 964.1 jit_solution(17502725451256504966)
XLA Ops:
  11.2 11.5 %all-to-all-start = ((s32[128,1,2]{2,1,0:T(1,128)}), s32[128,1,2]{2,1,0:T(1,128)S(1)}, u32[]{:S(2)}, u32[]{:S(2)}) async-start(s32[128,1,2]{2,1,0:T(1,128)} %bitcast.5), calls=%async_computation | async-start | bytes 131072 | tf_op jit(solution)/shard_map/all_to_all | solution.py:100
  27.0 8.6 gather_fusion.1
  35.6 9.8 %all-to-all-start.1 = ((s32[128,2,2,128]{3,1,2,0:T(2,128)}), s32[128,2,2,128]{3,1,2,0:T(2,128)S(1)}, u32[]{:S(2)}, u32[]{:S(2)}) async-start(s32[128,2,2,128]{3,1,2,0:T(2,128)} %pad_add_fusion), calls=%async_computation.1 | async-start | bytes 524288 | tf_op jit(solution)/shard_map/all_to_all | solution.py:93
  45.3 7.4 select_select_fusion
  52.8 3.5 all-to-all-done.1
  56.3 6.7 all-to-all-start.2
  63.1 20.7 %copy.55 = f32[1,1024,1,2048]{1,3,2,0:T(8,128)} copy(f32[1,1024,1,2048]{3,2,1,0:T(1,128)} %param.22) | data formatting | bytes 16777216 | tf_op args[0]
  85.4 78.2 %all-to-all-done.2 = bf16[128,2,128,128]{3,2,1,0:T(8,128)(2,1)} async-done(((bf16[128,2,128,128]{3,2,1,0:T(8,128)(2,1)}), bf16[128,2,128,128]{3,2,1,0:T(8,128)(2,1)}, u32[]{:S(2)}, u32[]{:S(2)}) %all-to-all-start.2) | async-done | bytes 8388640 | tf_op jit(solution)/shard_map/all_to_all | solution.py:86
  163.6 13.1 %fusion.8 = bf16[128,2,128,128]{3,2,1,0:T(8,128)(2,1)} fusion(s32[128,2,128]{2,1,0:T(2,128)S(1)} %get-tuple-element.125, bf16[128,2,128,128]{3,2,1,0:T(8,128)(2,1)} %all-to-all-done.2, s32[128,2,128]{2,1,0:T(2,128)S(1)} %get-tuple-element.124), kind=kOutput, calls=%fused_computation.24 | convolution fusion | flops 2164260864 | bytes 17039360 | tf_op jit(solution)/shard_map/abxj,abyj->abxy/dot_general | solution.py:40
  176.8 35.3 %copy.100 = bf16[32,8,128,128]{3,1,2,0:T(8,128)(2,1)} copy(bf16[32,8,128,128]{3,2,1,0:T(8,128)(2,1)} %bitcast.183) | data formatting | bytes 16777216
  212.0 11.9 %copy.59 = bf16[16384,256]{1,0:T(8,128)(2,1)} copy(bf16[16384,256]{0,1:T(8,128)(2,1)} %bitcast.179) | data formatting | bytes 16777216 | tf_op jit(solution)/shard_map/dot_general | solution.py:114
  223.9 6.2 fusion.83
  230.1 7.5 copy.99
  237.6 9.3 copy.60
  246.9 7.3 fusion.17
  258.1 34.0 %all_to_all.21 = bf16[8,1024,128]{1,2,0:T(8,128)(2,1)} all-to-all(bf16[8,1024,128]{1,2,0:T(8,128)(2,1)S(1)} %stack.26), channel_id=1, replica_groups=mesh['frow'=16,'fcol'=8] {'fcol'}, dimensions={0} | all-to-all | bytes 4194304 | tf_op jit(solution)/shard_map/all_to_all | solution.py:15
  292.1 5.2 collective-permute-start.1
  297.2 2.9 collective-permute-start
  303.3 3.9 copy.63
  307.2 37.9 %collective-permute-done.1 = bf16[1024,1024]{0,1:T(8,128)(2,1)} collective-permute-done((bf16[1024,1024]{0,1:T(8,128)(2,1)}, bf16[1024,1024]{0,1:T(8,128)(2,1)}, u32[]{:S(2)}, u32[]{:S(2)}) %collective-permute-start.1) | collective-permute-done | bytes 2097184 | tf_op jit(solution)/shard_map/ppermute | solution.py:141
  345.1 136.6 %collective-permute-done = bf16[1024,1024]{0,1:T(8,128)(2,1)} collective-permute-done((bf16[1024,1024]{0,1:T(8,128)(2,1)}, bf16[1024,1024]{0,1:T(8,128)(2,1)}, u32[]{:S(2)}, u32[]{:S(2)}) %collective-permute-start) | collective-permute-done | bytes 2097184 | tf_op jit(solution)/shard_map/ppermute | solution.py:141
  481.7 4.5 broadcast_select_fusion.1
  486.2 4.0 copy.76
  490.1 4.0 copy.77
  494.1 4.6 pad_maximum_fusion.2
  498.8 10.9 %all-gather.3.cloned.1.call-done = bf16[16384,128]{0,1:T(8,128)(2,1)} async-done(((bf16[128,128]{0,1:T(8,128)(2,1)}), bf16[16384,128]{0,1:T(8,128)(2,1)}) %all-gather.3.cloned.1.call-update) | async-done | bytes 4194320 | tf_op jit(solution)/shard_map/all_gather | solution.py:154
  513.3 5.0 copy.64
  518.3 3.7 copy_bitcast_fusion.1
  527.3 11.7 %cholesky.286 = f32[128,128]{1,0:T(8,128)S(1)} custom-call(f32[128,128]{1,0:T(8,128)S(1)} %cholesky.426), custom_call_target="Cholesky" | custom-call | tf_op jit(solution)/shard_map/jit(cholesky)/cholesky | solution.py:167
  539.1 9.8 %custom-call.27 = f32[1,128,128]{1,2,0:T(8,128)S(1)} custom-call(f32[1,128,128]{2,1,0:T(8,128)S(1)} %get-tuple-element.145), custom_call_target="InvertDiagBlocksLowerTriangular" | custom-call | tf_op jit(solution)/shard_map/jit(cholesky)/cholesky | solution.py:167
  551.6 11.7 %cholesky.305 = f32[128,128]{1,0:T(8,128)S(1)} custom-call(f32[128,128]{1,0:T(8,128)S(1)} %cholesky.430), custom_call_target="Cholesky" | custom-call | tf_op jit(solution)/shard_map/jit(cholesky)/cholesky | solution.py:167
  563.3 10.0 %custom-call.28 = f32[1,128,128]{1,2,0:T(8,128)S(1)} custom-call(f32[1,128,128]{2,1,0:T(8,128)S(1)} %get-tuple-element.142), custom_call_target="InvertDiagBlocksLowerTriangular" | custom-call | tf_op jit(solution)/shard_map/jit(cholesky)/cholesky | solution.py:167
  574.8 11.7 %cholesky.326 = f32[128,128]{1,0:T(8,128)S(1)} custom-call(f32[128,128]{1,0:T(8,128)S(1)} %cholesky.435), custom_call_target="Cholesky" | custom-call | tf_op jit(solution)/shard_map/jit(cholesky)/cholesky | solution.py:167
  587.3 9.8 %custom-call.29 = f32[1,128,128]{1,2,0:T(8,128)S(1)} custom-call(f32[1,128,128]{2,1,0:T(8,128)S(1)} %get-tuple-element.139), custom_call_target="InvertDiagBlocksLowerTriangular" | custom-call | tf_op jit(solution)/shard_map/jit(cholesky)/cholesky | solution.py:167
  598.5 12.1 %cholesky.343 = f32[128,128]{1,0:T(8,128)S(1)} custom-call(f32[128,128]{1,0:T(8,128)S(1)} %convolution_subtract_fusion.11), custom_call_target="Cholesky" | custom-call | tf_op jit(solution)/shard_map/jit(cholesky)/cholesky | solution.py:167
  615.9 11.9 %while.10 = (s32[]{:T(128)}, f32[512,512]{1,0:T(8,128)}, s32[4,2]{0,1:T(2,128)S(1)}, f32[4,128,128]{2,1,0:T(8,128)S(1)}, s32[]{:T(128)}) while((s32[]{:T(128)}, f32[512,512]{1,0:T(8,128)}, s32[4,2]{0,1:T(2,128)S(1)}, f32[4,128,128]{2,1,0:T(8,128)S(1)}, s32[]{:T(128)}) %tuple.86), condition=%wide.while_cond.6, body=%wide.while_body.6.sunk | while | flops 2 | bytes 131189 | solution.py:168
  616.5 2.3 bitcast_dynamic-update-slice_fusion.4
  619.5 2.3 bitcast_dynamic-update-slice_fusion.4
  622.5 2.3 bitcast_dynamic-update-slice_fusion.4
  627.7 39.3 %custom-call.30 = f32[4,128,128]{1,2,0:T(8,128)S(1)} custom-call(f32[4,128,128]{2,1,0:T(8,128)S(1)} %get-tuple-element.94), custom_call_target="InvertDiagBlocksLowerTriangular" | custom-call | tf_op jit(solution)/shard_map/triangular_solve/custom-call.3 | solution.py:168
  673.1 2.5 scatter.14
  675.6 3.1 constant_dynamic-update-slice_fusion.4
  678.8 4.1 broadcast_select_fusion.2
  689.7 11.7 %cholesky.358 = f32[128,128]{1,0:T(8,128)S(1)} custom-call(f32[128,128]{1,0:T(8,128)S(1)} %cholesky.439), custom_call_target="Cholesky" | custom-call | tf_op jit(solution)/shard_map/jit(cholesky)/cholesky | solution.py:167
  702.2 10.0 %custom-call.31 = f32[1,128,128]{1,2,0:T(8,128)S(1)} custom-call(f32[1,128,128]{2,1,0:T(8,128)S(1)} %get-tuple-element.135), custom_call_target="InvertDiagBlocksLowerTriangular" | custom-call | tf_op jit(solution)/shard_map/jit(cholesky)/cholesky | solution.py:167
  715.5 11.7 %cholesky.377 = f32[128,128]{1,0:T(8,128)S(1)} custom-call(f32[128,128]{1,0:T(8,128)S(1)} %cholesky.443), custom_call_target="Cholesky" | custom-call | tf_op jit(solution)/shard_map/jit(cholesky)/cholesky | solution.py:167
  727.9 9.8 %custom-call.32 = f32[1,128,128]{1,2,0:T(8,128)S(1)} custom-call(f32[1,128,128]{2,1,0:T(8,128)S(1)} %get-tuple-element.132), custom_call_target="InvertDiagBlocksLowerTriangular" | custom-call | tf_op jit(solution)/shard_map/jit(cholesky)/cholesky | solution.py:167
  740.9 11.7 %cholesky.398 = f32[128,128]{1,0:T(8,128)S(1)} custom-call(f32[128,128]{1,0:T(8,128)S(1)} %cholesky.448), custom_call_target="Cholesky" | custom-call | tf_op jit(solution)/shard_map/jit(cholesky)/cholesky | solution.py:167
  753.3 10.0 %custom-call.33 = f32[1,128,128]{1,2,0:T(8,128)S(1)} custom-call(f32[1,128,128]{2,1,0:T(8,128)S(1)} %get-tuple-element.129), custom_call_target="InvertDiagBlocksLowerTriangular" | custom-call | tf_op jit(solution)/shard_map/jit(cholesky)/cholesky | solution.py:167
  765.6 11.7 %cholesky.415 = f32[128,128]{1,0:T(8,128)S(1)} custom-call(f32[128,128]{1,0:T(8,128)S(1)} %convolution_subtract_fusion.10), custom_call_target="Cholesky" | custom-call | tf_op jit(solution)/shard_map/jit(cholesky)/cholesky | solution.py:167
  782.3 8.8 gather_fusion.2
  795.1 11.8 %while.11 = (s32[]{:T(128)}, f32[512,512]{1,0:T(8,128)}, s32[4,2]{0,1:T(2,128)S(1)}, f32[4,128,128]{2,1,0:T(8,128)S(1)}, s32[]{:T(128)}) while((s32[]{:T(128)}, f32[512,512]{1,0:T(8,128)}, s32[4,2]{0,1:T(2,128)S(1)}, f32[4,128,128]{2,1,0:T(8,128)S(1)}, s32[]{:T(128)}) %tuple.94), condition=%wide.while_cond.6.clone, body=%wide.while_body.6.clone.sunk | while | flops 2 | bytes 131189 | solution.py:168
  795.7 2.3 bitcast_dynamic-update-slice_fusion.5
  798.7 2.3 bitcast_dynamic-update-slice_fusion.5
  801.7 2.3 bitcast_dynamic-update-slice_fusion.5
  804.7 2.2 bitcast_dynamic-update-slice_fusion.5
  806.9 39.7 %custom-call.34 = f32[4,128,128]{1,2,0:T(8,128)S(1)} custom-call(f32[4,128,128]{2,1,0:T(8,128)S(1)} %get-tuple-element.95), custom_call_target="InvertDiagBlocksLowerTriangular" | custom-call | tf_op jit(solution)/shard_map/triangular_solve/custom-call.3 | solution.py:168
  855.9 7.0 fusion.21
  863.0 21.5 %fusion.149 = f32[3072,512]{1,0:T(8,128)S(1)} fusion(f32[3072,512]{0,1:T(8,128)S(1)} %fusion.21, f32[512,512]{1,0:T(8,128)S(1)} %get-tuple-element.153), kind=kOutput, calls=%fused_computation.282 | convolution fusion | flops 9663676416 | bytes 13631488 | tf_op jit(solution)/shard_map/dot_general | solution.py:186
  884.5 12.4 %fusion.11 = f32[3072,512]{0,1:T(8,128)S(1)} fusion(f32[3072,512]{1,0:T(8,128)S(1)} %fusion.149, bf16[2048,1024]{1,0:T(8,128)(2,1)} %bitcast.182, bf16[1024,1024]{1,0:T(8,128)(2,1)S(1)} %copy-done.3, f32[128,512]{1,0:T(8,128)S(1)} %fusion.86, f32[128,512]{1,0:T(8,128)S(1)} %copy-done.12, f32[128,512]{1,0:T(8,128)S(1)} %copy-done.6, f32[128,512]{1,0:T(8,128)S(1)} %fusion.65), kind=kOutput, calls=%fused_computation.27 | convolution fusion | flops 9673900032 | bytes 19922944 | tf_op jit(solution)/shard_map/dot_general | solution.py:170
  897.0 30.5 %fusion.16 = f32[1024,2048]{0,1:T(8,128)} fusion(f32[1024,2048]{0,1:T(8,128)} %copy.60, f32[1,1024,1,2048]{1,3,2,0:T(8,128)S(1)} %bitcast.177, f32[3072,512]{0,1:T(8,128)S(1)} %fusion.11, f32[3072,512]{0,1:T(8,128)S(1)} %fusion.21), kind=kOutput, calls=%fused_computation.33 | convolution fusion | flops 25777143808 | bytes 37748736 | tf_op jit(solution)/shard_map/dot_general | solution.py:47
  927.5 2.8 fusion.55
  930.3 5.9 select_bitcast_fusion
  936.3 20.5 %copy.73 = f32[1,1024,1,2048]{3,2,1,0:T(1,128)} copy(f32[1,1024,1,2048]{1,3,2,0:T(8,128)} %select_bitcast_fusion) | data formatting | bytes 16777216 | tf_op jit(solution)/shard_map/broadcast_in_dim | solution.py:199
  (178 shorter events, 82.4 us)
Async XLA Ops:
  6.5 20.5 %copy-start = (bf16[64,128,128]{2,1,0:T(8,128)(2,1)S(1)}, bf16[64,128,128]{2,1,0:T(8,128)(2,1)}, u32[]{:S(2)}) copy-start(bf16[64,128,128]{2,1,0:T(8,128)(2,1)} %param.23) | copy-start | bytes 6291460
  11.2 24.4 %all-to-all-start = ((s32[128,1,2]{2,1,0:T(1,128)}), s32[128,1,2]{2,1,0:T(1,128)S(1)}, u32[]{:S(2)}, u32[]{:S(2)}) async-start(s32[128,1,2]{2,1,0:T(1,128)} %bitcast.5), calls=%async_computation | async-start | bytes 131072 | tf_op jit(solution)/shard_map/all_to_all | solution.py:100
  35.6 20.7 %all-to-all-start.1 = ((s32[128,2,2,128]{3,1,2,0:T(2,128)}), s32[128,2,2,128]{3,1,2,0:T(2,128)S(1)}, u32[]{:S(2)}, u32[]{:S(2)}) async-start(s32[128,2,2,128]{3,1,2,0:T(2,128)} %pad_add_fusion), calls=%async_computation.1 | async-start | bytes 524288 | tf_op jit(solution)/shard_map/all_to_all | solution.py:93
  56.3 107.4 %all-to-all-start.2 = ((bf16[128,2,128,128]{3,2,1,0:T(8,128)(2,1)}), bf16[128,2,128,128]{3,2,1,0:T(8,128)(2,1)}, u32[]{:S(2)}, u32[]{:S(2)}) async-start(bf16[128,2,128,128]{3,2,1,0:T(8,128)(2,1)} %select_select_fusion), calls=%async_computation.2 | async-start | bytes 16777216 | tf_op jit(solution)/shard_map/all_to_all | solution.py:86
  63.0 446.6 %all-gather.3.cloned.1.call-start = ((), (), s32[]{:S(2)}) async-start(), calls=%async_computation.4 | async-start | bytes 4227072 | tf_op jit(solution)/shard_map/all_gather | solution.py:154
  254.2 2.0 copy-start.4
  292.1 53.1 %collective-permute-start.1 = (bf16[1024,1024]{0,1:T(8,128)(2,1)}, bf16[1024,1024]{0,1:T(8,128)(2,1)}, u32[]{:S(2)}, u32[]{:S(2)}) collective-permute-start(bf16[1024,1024]{0,1:T(8,128)(2,1)} %bitcast.20), channel_id=1, source_target_pairs={{0,0},{1,8},{2,16},{3,24},{4,32},{5,40},{6,48},{7,56},{8,1},{9,9},... | collective-permute-start | bytes 6291464 | tf_op jit(solution)/shard_map/ppermute | solution.py:141
  297.2 184.5 %collective-permute-start = (bf16[1024,1024]{0,1:T(8,128)(2,1)}, bf16[1024,1024]{0,1:T(8,128)(2,1)}, u32[]{:S(2)}, u32[]{:S(2)}) collective-permute-start(bf16[1024,1024]{0,1:T(8,128)(2,1)} %bitcast.20), channel_id=1, source_target_pairs={{0,64},{1,72},{2,80},{3,88},{4,96},{5,104},{6,112},{7,120},{8,65},... | collective-permute-start | bytes 6291464 | tf_op jit(solution)/shard_map/ppermute | solution.py:141
  522.0 1.9 copy-start.2
  526.4 1.0 copy-start.10
  669.1 9.6 copy-start.7
  669.1 9.6 copy-start.17
  671.0 11.9 %copy-start.13 = (f32[128,512]{1,0:T(8,128)}, f32[128,512]{1,0:T(8,128)S(1)}, u32[]{:S(2)}) copy-start(f32[128,512]{1,0:T(8,128)S(1)} %fusion.93) | copy-start | bytes 786436
  673.1 9.8 %copy-start.16 = (f32[128,512]{1,0:T(8,128)}, f32[128,512]{1,0:T(8,128)S(1)}, u32[]{:S(2)}) copy-start(f32[128,512]{1,0:T(8,128)S(1)} %fusion.92) | copy-start | bytes 786436
  688.7 1.0 copy-start.9
  714.8 0.7 copy-start.18
  740.2 0.7 copy-start.19
  791.1 64.8 %copy-start.8 = (f32[128,512]{1,0:T(8,128)S(1)}, f32[128,512]{1,0:T(8,128)}, u32[]{:S(2)}) copy-start(f32[128,512]{1,0:T(8,128)} %copy-done.7) | copy-start | bytes 786436
  791.1 64.8 %copy-start.14 = (f32[128,512]{1,0:T(8,128)S(1)}, f32[128,512]{1,0:T(8,128)}, u32[]{:S(2)}) copy-start(f32[128,512]{1,0:T(8,128)} %copy-done.13) | copy-start | bytes 786436
  846.6 0.7 copy-start.20
  850.2 5.6 copy-start.5
  852.9 2.9 copy-start.11
  862.9 21.5 %copy-start.3 = (bf16[1024,1024]{1,0:T(8,128)(2,1)S(1)}, bf16[1024,1024]{1,0:T(8,128)(2,1)}, u32[]{:S(2)}) copy-start(bf16[1024,1024]{1,0:T(8,128)(2,1)} %copy.63) | copy-start | bytes 6291460
  862.9 21.5 %copy-start.6 = (f32[128,512]{1,0:T(8,128)S(1)}, f32[128,512]{1,0:T(8,128)}, u32[]{:S(2)}) copy-start(f32[128,512]{1,0:T(8,128)} %copy-done.5) | copy-start | bytes 786436
  862.9 21.5 %copy-start.12 = (f32[128,512]{1,0:T(8,128)S(1)}, f32[128,512]{1,0:T(8,128)}, u32[]{:S(2)}) copy-start(f32[128,512]{1,0:T(8,128)} %copy-done.11) | copy-start | bytes 786436
  862.9 34.0 %slice-start = ((s8[8388608]{0:T(1024)(128)(4,1)}), s8[4194304]{0:T(1024)(128)(4,1)S(1)}, s32[]{:S(2)}) async-start(s8[8388608]{0:T(1024)(128)(4,1)} %bitcast.176), calls=%async_computation.5 | async-start | bytes 8388608
  884.5 12.4 %slice-start.1 = ((s8[8388608]{0:T(1024)(128)(4,1)}), s8[4194304]{0:T(1024)(128)(4,1)S(1)}, s32[]{:S(2)}) async-start(s8[8388608]{0:T(1024)(128)(4,1)} %bitcast.176), calls=%async_computation.6 | async-start | bytes 8388608
  897.0 30.6 %copy-start.15 = (f32[1024,128]{0,1:T(8,128)S(1)}, f32[1024,128]{0,1:T(8,128)}, u32[]{:S(2)}) copy-start(f32[1024,128]{0,1:T(8,128)} %copy.89) | copy-start | bytes 1572868
  897.0 30.5 %copy-start.21 = (pred[1024]{0:T(1024)(128)(4,1)S(1)}, pred[1024]{0:T(1024)(128)(4,1)}, u32[]{:S(2)}) copy-start(pred[1024]{0:T(1024)(128)(4,1)} %get-tuple-element.158) | copy-start | bytes 3076
  897.0 30.5 %copy-start.22 = (pred[1024]{0:T(1024)(128)(4,1)S(1)}, pred[1024]{0:T(1024)(128)(4,1)}, u32[]{:S(2)}) copy-start(pred[1024]{0:T(1024)(128)(4,1)} %get-tuple-element.159) | copy-start | bytes 3076
  930.3 26.4 %copy-start.1 = (bf16[64,128,128]{2,1,0:T(8,128)(2,1)S(1)}, bf16[64,128,128]{2,1,0:T(8,128)(2,1)}, u32[]{:S(2)}) copy-start(bf16[64,128,128]{2,1,0:T(8,128)(2,1)} %param.23) | copy-start | bytes 6291460
Sparse Core Ops, SparseCore 0:
  257.0 252.6 all-gather.2
